TPU v7x, 256 devices: a whole 4x4x8 slice. The times are simulated.
256 devices in a mesh: blk: 8 (over y_lo, x), wide: 32 (over y_hi, z, core).
Axes of the slice: x: 4, y: 4 (y_hi: 2, y_lo: 2; y = y_hi * 2 + y_lo), z: 8, core: 2. Of those that a mesh axis runs over, the one named last changes fastest.
Arguments:
- a_blocks: float32 [32, 8, 32, 4, 128, 128], P('blk', None, 'wide'), may hold values from -6 to 6
- a_map: int32 [32, 8, 32, 4], P('blk', None, 'wide'), may hold values 0 or 1
- b_blocks: float32 [8, 32, 4, 8, 128, 128], P('blk', 'wide'), may hold values from -0.03125 to 0.03125
- b_map: int32 [8, 32, 4, 8], P('blk', 'wide'), may hold values 0 or 1
- owner_map: int32 [32, 8], P('blk'), may hold values from -1 to 31, as said below
Outputs:
- owned: float32 [8, 32, 2, 128, 128], P('blk', 'wide')
Inputs may be any that keep to these rules, and one draw needn't show every extreme that they name: `owner_map`: in each panel of 4 x 8 product blocks (block rows i * 4 to i * 4 + 3), each owner holds at most 2 blocks, and one owner holds exactly 2.
All inputs are finite; a program needn't handle non-finite values. No bound on the sum of `a_map` or of `b_map` on one device may be relied on, other than what follows from the above.
Results may differ from a plain program's by a relative error of at most 0.00007.
Values sent between devices are 32-bit elements; how exact they have to be, the bound alone decides.
No kernel may reach another device: no remote copies, remote signals or barrier semaphores. Data moves between devices by JAX's collectives and lax.ppermute only.
A program may use at most 128 MiB of HBM per device.

v0:
```python
import jax
import jax.numpy as jnp
from jax import lax
from jax.sharding import PartitionSpec as P


def shifted(value, axis, by):
    devices = lax.axis_size(axis)
    return lax.ppermute(value, axis, [(i, (i + by) % devices) for i in range(devices)])


def per_device(a_blocks, a_map, b_blocks, b_map, owner_map):
    highest = lax.Precision.HIGHEST
    cycle_size = lax.axis_size("blk")
    wide_size = lax.axis_size("wide")
    myself = lax.axis_index("blk")
    left_used = a_blocks[:, :, 0] * a_map[:, :, 0, :, None, None].astype(jnp.float32)
    right_used = b_blocks[0, 0] * b_map[0, 0][:, :, None, None].astype(jnp.float32)
    rows_here, cols_here = owner_map.shape
    block_side = right_used.shape[-1]
    partial_value = jnp.zeros((rows_here, cols_here, block_side, block_side), jnp.float32)
    panel = right_used
    for turn_index in range(cycle_size):
        left_panel = lax.dynamic_index_in_dim(
            left_used, (myself - turn_index) % cycle_size, 1, keepdims=False
        )
        partial_value = partial_value + jnp.einsum(
            "rtxy,tcyz->rcxz", left_panel, panel, precision=highest
        )
        if turn_index + 1 < cycle_size:
            panel = shifted(panel, "blk", 1)
    block_count = rows_here * cols_here
    slots_each = max(2, 2 * block_count // wide_size)
    owner_list = owner_map.reshape(block_count)
    owner_hit = (owner_list[:, None] == jnp.arange(wide_size, dtype=jnp.int32)[None, :]).astype(
        jnp.int32
    )
    slot_rank = jnp.cumsum(owner_hit, axis=0) - owner_hit
    slot_match = (slot_rank[:, :, None] == jnp.arange(slots_each, dtype=jnp.int32)).astype(
        jnp.int32
    )
    selector = (owner_hit[:, :, None] * slot_match).astype(jnp.float32)
    outgoing = jnp.einsum(
        "qos,qxy->osxy",
        selector,
        partial_value.reshape(block_count, block_side, block_side),
        precision=highest,
    )
    arrived = lax.all_to_all(outgoing, "wide", split_axis=0, concat_axis=0, tiled=True)
    owned_blocks = jnp.sum(arrived, axis=0)
    return owned_blocks[None, None]


def solution(mesh):
    in_specs = (
        P("blk", None, "wide", None, None, None),
        P("blk", None, "wide", None),
        P("blk", "wide", None, None, None, None),
        P("blk", "wide", None, None),
        P("blk", None),
    )
    out_specs = P("blk", "wide", None, None, None)
    return jax.shard_map(
        per_device, mesh=mesh, in_specs=in_specs, out_specs=out_specs, check_vma=False
    )
```

profile of v0, /device:TPU:32, one launch (start us, length us, event | category | flops | bytes accessed | tf_op | source)
XLA Modules:
  0.0 466.6 jit_solution(18118034099545313763)
XLA Ops:
  0.0 0.7 convert_bitcast_fusion.1
  0.7 0.1 copy.25
  0.8 1.9 copy.24
  2.7 0.0 copy-start.10
  2.7 0.0 copy-start.9
  2.7 0.2 bitcast_multiply_fusion.1
  2.9 1.6 collective-permute-start
  4.5 48.0 %collective-permute-done = f32[4,8,128,128]{2,3,0,1:T(8,128)S(1)} collective-permute-done((f32[4,8,128,128]{2,3,0,1:T(8,128)S(1)}, f32[4,8,128,128]{2,3,0,1:T(8,128)S(1)}, u32[]{:S(2)}, u32[]{:S(2)}) %collective-permute-start) | collective-permute-done | bytes 2097184 | tf_op jit(solution)/shard_map/ppermute | solution.py:9
  52.5 1.3 copy-done.3
  53.8 0.0 collective-permute-start.1
  53.8 48.6 %collective-permute-done.1 = f32[4,8,128,128]{2,3,0,1:T(8,128)S(1)} collective-permute-done((f32[4,8,128,128]{2,3,0,1:T(8,128)S(1)}, f32[4,8,128,128]{2,3,0,1:T(8,128)S(1)}, u32[]{:S(2)}, u32[]{:S(2)}) %collective-permute-start.1) | collective-permute-done | bytes 2097184 | tf_op jit(solution)/shard_map/ppermute | solution.py:9
  102.4 1.3 copy-done.4
  103.8 0.0 collective-permute-start.2
  103.8 47.8 %collective-permute-done.2 = f32[4,8,128,128]{2,3,0,1:T(8,128)S(1)} collective-permute-done((f32[4,8,128,128]{2,3,0,1:T(8,128)S(1)}, f32[4,8,128,128]{2,3,0,1:T(8,128)S(1)}, u32[]{:S(2)}, u32[]{:S(2)}) %collective-permute-start.2) | collective-permute-done | bytes 2097184 | tf_op jit(solution)/shard_map/ppermute | solution.py:9
  151.5 1.3 copy-done.5
  152.8 0.0 collective-permute-start.3
  152.8 46.9 %collective-permute-done.3 = f32[4,8,128,128]{2,3,0,1:T(8,128)S(1)} collective-permute-done((f32[4,8,128,128]{2,3,0,1:T(8,128)S(1)}, f32[4,8,128,128]{2,3,0,1:T(8,128)S(1)}, u32[]{:S(2)}, u32[]{:S(2)}) %collective-permute-start.3) | collective-permute-done | bytes 2097184 | tf_op jit(solution)/shard_map/ppermute | solution.py:9
  199.7 1.3 copy-done.7
  201.0 0.0 collective-permute-start.4
  201.0 46.2 %collective-permute-done.4 = f32[4,8,128,128]{2,3,0,1:T(8,128)} collective-permute-done((f32[4,8,128,128]{2,3,0,1:T(8,128)S(1)}, f32[4,8,128,128]{2,3,0,1:T(8,128)}, u32[]{:S(2)}, u32[]{:S(2)}) %collective-permute-start.4) | collective-permute-done | bytes 2097184 | tf_op jit(solution)/shard_map/ppermute | solution.py:9
  247.2 0.3 collective-permute-start.5
  247.6 0.0 copy-done.10
  247.7 0.1 eq.48
  247.7 0.1 fusion.44
  247.8 0.1 copy.21
  247.9 0.1 reduce_window_sum.11
  247.9 0.0 copy-done.9
  248.0 0.1 copy.22
  248.1 4.1 bitcast_multiply_fusion
  252.2 3.2 copy-done
  255.4 6.8 %fusion.17 = f32[8,128,4,128,1]{3,1,4,2,0:T(8,128)S(1)} fusion(f32[4,8,4,128,128]{4,3,2,1,0:T(8,128)S(1)} %bitcast_multiply_fusion, s32[]{:T(128)S(6)} %select_n.61, f32[1,1,4,8,128,128]{5,4,3,2,1,0:T(8,128)S(1)} %copy-done.2, f32[4,8]{1,0:T(4,128)S(1)} %convert_bitcast_fusion.1), kind=kOutput, calls=%fused_computation.26 | convolution fusion | flops 3221749760 | bytes 5244932 | tf_op jit(solution)/shard_map/rtxy,tcyz->rcxz/dot_general | solution.py:27
  262.2 30.8 %collective-permute-done.5 = f32[4,8,128,128]{2,3,0,1:T(8,128)} collective-permute-done((f32[4,8,128,128]{2,3,0,1:T(8,128)}, f32[4,8,128,128]{2,3,0,1:T(8,128)}, u32[]{:S(2)}, u32[]{:S(2)}) %collective-permute-start.5) | collective-permute-done | bytes 2097184 | tf_op jit(solution)/shard_map/ppermute | solution.py:9
  293.0 0.5 collective-permute-start.6
  293.5 0.1 fusion.45
  293.6 0.1 copy.20
  293.7 5.5 %fusion.12 = f32[8,128,4,128,1]{3,1,4,2,0:T(8,128)S(1)} fusion(f32[4,8,128,128]{2,3,0,1:T(8,128)} %copy-done.3, f32[4,8,4,128,128]{4,3,2,1,0:T(8,128)} %copy-done, s32[]{:T(128)S(6)} %select_n.63), kind=kOutput, calls=%fused_computation.13 | convolution fusion | flops 3221225472 | bytes 5242884 | tf_op jit(solution)/shard_map/rtxy,tcyz->rcxz/dot_general | solution.py:27
  299.2 5.5 %fusion.10 = f32[8,128,4,128,1]{3,1,4,2,0:T(8,128)S(1)} fusion(f32[4,8,128,128]{2,3,0,1:T(8,128)} %copy-done.4, f32[4,8,4,128,128]{4,3,2,1,0:T(8,128)} %copy-done, s32[]{:T(128)S(6)} %select_n.65), kind=kOutput, calls=%fused_computation.11 | convolution fusion | flops 3221225472 | bytes 5242884 | tf_op jit(solution)/shard_map/rtxy,tcyz->rcxz/dot_general | solution.py:27
  304.7 3.5 fusion.8
  308.2 3.7 fusion.6
  311.9 5.1 %fusion.4 = f32[8,128,4,128,1]{3,1,4,2,0:T(8,128)S(1)} fusion(f32[4,8,128,128]{2,3,0,1:T(8,128)} %collective-permute-done.4, f32[4,8,4,128,128]{4,3,2,1,0:T(8,128)S(1)} %copy-done.1, s32[]{:T(128)S(6)} %select_n.71), kind=kOutput, calls=%fused_computation.5 | convolution fusion | flops 3221225472 | bytes 5242884 | tf_op jit(solution)/shard_map/rtxy,tcyz->rcxz/dot_general | solution.py:27
  317.0 5.1 %fusion.2 = f32[8,128,4,128,1]{3,1,4,2,0:T(8,128)S(1)} fusion(f32[4,8,128,128]{2,3,0,1:T(8,128)} %collective-permute-done.5, f32[4,8,4,128,128]{4,3,2,1,0:T(8,128)S(1)} %copy-done.1, s32[]{:T(128)S(6)} %select_n.73), kind=kOutput, calls=%fused_computation.3 | convolution fusion | flops 3221225472 | bytes 5242884 | tf_op jit(solution)/shard_map/rtxy,tcyz->rcxz/dot_general | solution.py:27
  322.1 16.1 %collective-permute-done.6 = f32[4,8,128,128]{2,3,0,1:T(8,128)} collective-permute-done((f32[4,8,128,128]{2,3,0,1:T(8,128)}, f32[4,8,128,128]{2,3,0,1:T(8,128)}, u32[]{:S(2)}, u32[]{:S(2)}) %collective-permute-start.6) | collective-permute-done | bytes 2097184 | tf_op jit(solution)/shard_map/ppermute | solution.py:9
  338.2 7.1 %fusion.16 = f32[4,8,128,128]{2,3,0,1:T(8,128)} fusion(f32[8,128,4,128,1]{3,1,4,2,0:T(8,128)S(1)} %fusion.2, f32[8,128,4,128,1]{3,1,4,2,0:T(8,128)S(1)} %fusion.4, f32[8,128,4,128,1]{3,1,4,2,0:T(8,128)S(1)} %fusion.6, f32[8,128,4,128,1]{3,1,4,2,0:T(8,128)S(1)} %fusion.8, f32[8,128,4,128,1]{3,1,4,2,0:T(8,128)S(1)} %fusion.10, ...), kind=kOutput, calls=%fused_computation.18 | convolution fusion | flops 3224895488 | bytes 19922948 | tf_op jit(solution)/shard_map/rtxy,tcyz->rcxz/dot_general | solution.py:27
  345.2 1.9 copy.26
  347.2 4.6 fusion.14
  351.7 2.4 copy.28
  354.2 109.1 %all_to_all.5 = f32[32,2,128,128]{3,2,1,0:T(8,128)} all-to-all(f32[32,2,128,128]{3,2,1,0:T(8,128)S(1)} %copy.28), channel_id=1, replica_groups=mesh['blk'=8,'wide'=32] {'wide'}, dimensions={0} | all-to-all | bytes 8388608 | tf_op jit(solution)/shard_map/all_to_all | solution.py:49
  463.3 3.0 reduce_sum.9
  (14 shorter events, 0.0 us)
Async XLA Ops:
  2.7 244.9 %copy-start.10 = (s32[4,8]{1,0:T(4,128)S(1)}, s32[4,8]{1,0:T(4,128)}, u32[]{:S(2)}) copy-start(s32[4,8]{1,0:T(4,128)} %param.9) | copy-start | bytes 388
  2.7 245.2 %copy-start.9 = (s32[4,8,1,4]{1,3,2,0:T(4,128)S(1)}, s32[4,8,1,4]{1,3,2,0:T(4,128)}, u32[]{:S(2)}) copy-start(s32[4,8,1,4]{1,3,2,0:T(4,128)} %param.6) | copy-start | bytes 1540
  2.9 49.6 %collective-permute-start = (f32[4,8,128,128]{2,3,0,1:T(8,128)S(1)}, f32[4,8,128,128]{2,3,0,1:T(8,128)S(1)}, u32[]{:S(2)}, u32[]{:S(2)}) collective-permute-start(f32[4,8,128,128]{2,3,0,1:T(8,128)S(1)} %bitcast_multiply_fusion.1), channel_id=1, source_target_pairs={{0,32},{32,64},{64,96},{96,128},{128,160},{160,192},{192,224},{224... | collective-permute-start | bytes 6291464 | tf_op jit(solution)/shard_map/ppermute | solution.py:9
  52.5 1.3 copy-start.3
  53.8 48.6 %collective-permute-start.1 = (f32[4,8,128,128]{2,3,0,1:T(8,128)S(1)}, f32[4,8,128,128]{2,3,0,1:T(8,128)S(1)}, u32[]{:S(2)}, u32[]{:S(2)}) collective-permute-start(f32[4,8,128,128]{2,3,0,1:T(8,128)S(1)} %collective-permute-done), channel_id=1, source_target_pairs={{0,32},{32,64},{64,96},{96,128},{128,160},{160,192},{192,224},{224... | collective-permute-start | bytes 6291464 | tf_op jit(solution)/shard_map/ppermute | solution.py:9
  102.4 1.3 copy-start.4
  103.8 47.8 %collective-permute-start.2 = (f32[4,8,128,128]{2,3,0,1:T(8,128)S(1)}, f32[4,8,128,128]{2,3,0,1:T(8,128)S(1)}, u32[]{:S(2)}, u32[]{:S(2)}) collective-permute-start(f32[4,8,128,128]{2,3,0,1:T(8,128)S(1)} %collective-permute-done.1), channel_id=1, source_target_pairs={{0,32},{32,64},{64,96},{96,128},{128,160},{160,192},{192,224},{224... | collective-permute-start | bytes 6291464 | tf_op jit(solution)/shard_map/ppermute | solution.py:9
  151.5 1.3 copy-start.5
  152.8 46.9 %collective-permute-start.3 = (f32[4,8,128,128]{2,3,0,1:T(8,128)S(1)}, f32[4,8,128,128]{2,3,0,1:T(8,128)S(1)}, u32[]{:S(2)}, u32[]{:S(2)}) collective-permute-start(f32[4,8,128,128]{2,3,0,1:T(8,128)S(1)} %collective-permute-done.2), channel_id=1, source_target_pairs={{0,32},{32,64},{64,96},{96,128},{128,160},{160,192},{192,224},{224... | collective-permute-start | bytes 6291464 | tf_op jit(solution)/shard_map/ppermute | solution.py:9
  199.7 1.3 copy-start.7
  201.0 46.2 %collective-permute-start.4 = (f32[4,8,128,128]{2,3,0,1:T(8,128)S(1)}, f32[4,8,128,128]{2,3,0,1:T(8,128)}, u32[]{:S(2)}, u32[]{:S(2)}) collective-permute-start(f32[4,8,128,128]{2,3,0,1:T(8,128)S(1)} %collective-permute-done.3), channel_id=1, source_target_pairs={{0,32},{32,64},{64,96},{96,128},{128,160},{160,192},{192,224},{224... | collective-permute-start | bytes 6291464 | tf_op jit(solution)/shard_map/ppermute | solution.py:9
  247.2 45.8 %collective-permute-start.5 = (f32[4,8,128,128]{2,3,0,1:T(8,128)}, f32[4,8,128,128]{2,3,0,1:T(8,128)}, u32[]{:S(2)}, u32[]{:S(2)}) collective-permute-start(f32[4,8,128,128]{2,3,0,1:T(8,128)} %collective-permute-done.4), channel_id=1, source_target_pairs={{0,32},{32,64},{64,96},{96,128},{128,160},{160,192},{192,224},{224... | collective-permute-start | bytes 6291464 | tf_op jit(solution)/shard_map/ppermute | solution.py:9
  248.1 7.4 %copy-start.2 = (f32[1,1,4,8,128,128]{5,4,3,2,1,0:T(8,128)S(1)}, f32[1,1,4,8,128,128]{5,4,3,2,1,0:T(8,128)}, u32[]{:S(2)}) copy-start(f32[1,1,4,8,128,128]{5,4,3,2,1,0:T(8,128)} %param.7) | copy-start | bytes 6291460
  252.2 3.2 copy-start
  293.0 45.2 %collective-permute-start.6 = (f32[4,8,128,128]{2,3,0,1:T(8,128)}, f32[4,8,128,128]{2,3,0,1:T(8,128)}, u32[]{:S(2)}, u32[]{:S(2)}) collective-permute-start(f32[4,8,128,128]{2,3,0,1:T(8,128)} %collective-permute-done.5), channel_id=1, source_target_pairs={{0,32},{32,64},{64,96},{96,128},{128,160},{160,192},{192,224},{224... | collective-permute-start | bytes 6291464 | tf_op jit(solution)/shard_map/ppermute | solution.py:9
  293.7 11.0 %copy-start.1 = (f32[4,8,4,128,128]{4,3,2,1,0:T(8,128)S(1)}, f32[4,8,4,128,128]{4,3,2,1,0:T(8,128)}, u32[]{:S(2)}) copy-start(f32[4,8,4,128,128]{4,3,2,1,0:T(8,128)} %copy-done) | copy-start | bytes 25165828
  299.2 5.5 %copy-start.6 = (f32[4,8,128,128]{2,3,0,1:T(8,128)S(1)}, f32[4,8,128,128]{2,3,0,1:T(8,128)}, u32[]{:S(2)}) copy-start(f32[4,8,128,128]{2,3,0,1:T(8,128)} %copy-done.5) | copy-start | bytes 6291460
  304.7 3.5 copy-start.8
where the time goes:
time: 471 us; the launch traced here: 467 us
  waiting for transfers between devices  284 us (60%)
  blocking collectives  109 us (23%)
  matrix products  46.7 us (10%)
  local copies, waits for them, and re-layouts  15.2 us (3%)
  other arithmetic  8.28 us (2%)
    ppermute x7, waiting for transfers between devices, shifted(): lax.ppermute(value, axis, [(i, (i + by) % devices) for i in range(devices)])  284 us
    all_to_all x1, blocking collectives, per_device(): lax.all_to_all(outgoing, 'wide', split_axis=0, concat_axis=0, tiled=True)  109 us
    dot_general x8, matrix products, per_device(): jnp.einsum('rtxy,tcyz->rcxz', left_panel, panel, precision=highest)  42.2 us
    unnamed x23, local copies, waits for them, and re-layouts  10.4 us
  transfers between devices with their start and end apart: 7, of which 7 were waited for; matrix products, arithmetic and copies ran while one was open for 9% of the time, Pallas kernels for 0%

commit v1 on v0

v1 whole, which is shorter than its diff:
```python
import jax
import jax.numpy as jnp
from jax import lax
from jax.sharding import PartitionSpec as P


def moved(value, axis, target):
    devices = lax.axis_size(axis)
    return lax.ppermute(value, axis, [(i, target(i)) for i in range(devices)])


def per_device(a_blocks, a_map, b_blocks, b_map, owner_map, row_len):
    highest = lax.Precision.HIGHEST
    cycle_size = lax.axis_size("blk")
    wide_size = lax.axis_size("wide")
    n_rows = cycle_size // row_len
    myself = lax.axis_index("blk")
    me_wide = lax.axis_index("wide")
    row = myself // row_len
    col = myself % row_len
    other_row = (row + 1) % n_rows

    def right(i):
        return (i // row_len) * row_len + (i % row_len + 1) % row_len

    def left(i):
        return (i // row_len) * row_len + (i % row_len - 1) % row_len

    def partner(i):
        return (i + row_len) % cycle_size

    left_used = a_blocks[:, :, 0] * a_map[:, :, 0, :, None, None].astype(jnp.float32)
    right_used = b_blocks[0, 0] * b_map[0, 0][:, :, None, None].astype(jnp.float32)
    rows_here, cols_here = owner_map.shape
    block_side = right_used.shape[-1]
    half = cols_here // 2

    partner_left = {}
    for offset in (0, 1, row_len - 1, 2):
        sent = lax.dynamic_index_in_dim(
            left_used, other_row * row_len + (col + offset) % row_len, 1, keepdims=False
        )
        partner_left[offset] = moved(sent, "blk", partner)

    partner_owners = moved(owner_map, "blk", partner)

    from_right = moved(right_used, "blk", left)
    from_left = moved(right_used, "blk", right)
    far_low = moved(from_left[:, :half], "blk", right)
    far_high = moved(from_right[:, half:], "blk", left)

    def left_pair(offset):
        k = (col + offset) % row_len
        own = lax.dynamic_index_in_dim(left_used, row * row_len + k, 1, keepdims=False)
        return jnp.concatenate([own, partner_left[offset]], axis=0)

    def product(lhs, rhs):
        return jnp.einsum("rtxy,tcyz->rcxz", lhs, rhs, precision=highest)

    partial_value = product(left_pair(0), right_used)
    partial_value = partial_value + product(left_pair(1), from_right)
    partial_value = partial_value + product(left_pair(row_len - 1), from_left)
    far = left_pair(2)
    partial_value = partial_value + jnp.concatenate(
        [product(far, far_low), product(far, far_high)], axis=1
    )

    block_count = rows_here * cols_here
    stacked = partial_value.reshape(2, block_count, block_side, block_side)
    summed = lax.psum(stacked, "wide")

    def owned_slots(owner_list, panel):
        owner_hit = (owner_list == me_wide).astype(jnp.int32)
        slot_rank = jnp.cumsum(owner_hit) - owner_hit
        slots = []
        for slot in range(2):
            chosen = (owner_hit == 1) & (slot_rank == slot)
            index = jnp.argmax(chosen)
            taken = jnp.any(chosen)
            block = lax.dynamic_index_in_dim(panel, index, 0, keepdims=False)
            slots.append(jnp.where(taken, block, jnp.zeros_like(block)))
        return jnp.stack(slots)

    mine = owned_slots(owner_map.reshape(block_count), summed[0])
    for_partner = owned_slots(partner_owners.reshape(block_count), summed[1])
    slots = mine + moved(for_partner, "blk", partner)
    return slots[None, None]


def solution(mesh):
    in_specs = (
        P("blk", None, "wide", None, None, None),
        P("blk", None, "wide", None),
        P("blk", "wide", None, None, None, None),
        P("blk", "wide", None, None),
        P("blk", None),
    )
    out_specs = P("blk", "wide", None, None, None)
    row_len = 4

    def body(*args):
        return per_device(*args, row_len=row_len)

    return jax.shard_map(
        body, mesh=mesh, in_specs=in_specs, out_specs=out_specs, check_vma=False
    )
```

time: 471 us -> 425 us (0.902)
  blocking collectives: 109 us -> 0 us
  waiting for transfers between devices: 284 us -> 323 us
  between operations: 0.59 us -> 20.7 us
  matrix products: 46.7 us -> 33.4 us
  starting transfers between devices: 2.37 us -> 14.6 us
  other arithmetic: 8.28 us -> 13.2 us
    psum x0 -> x1, waiting for transfers between devices: none -> 266 us  [per_device(): summed = lax.psum(stacked, 'wide')]
    ppermute x7 -> x10, waiting for transfers between devices: 284 us -> 57.7 us  [moved(): return lax.ppermute(value, axis, [(i, target(i)) for i in range(devices)])]
    all_to_all x1 -> x0, blocking collectives: 109 us -> none  [per_device(): lax.all_to_all(outgoing, 'wide', split_axis=0, concat_axis=0, tiled=True)]
    dot_general x9 -> x5, matrix products: 46.7 us -> 33.4 us  [product(): return jnp.einsum('rtxy,tcyz->rcxz', lhs, rhs, precision=highest)]
    ppermute x7 -> x10, starting transfers between devices: 2.37 us -> 14.6 us  [moved(): return lax.ppermute(value, axis, [(i, target(i)) for i in range(devices)])]
    unnamed x23 -> x7, local copies, waits for them, and re-layouts: 10.4 us -> 2.6 us
  transfers between devices with their start and end apart: 7 -> 11, of which waited for: 7 -> 5; matrix products, arithmetic and copies ran while one was open for 9% -> 9% of each run, Pallas kernels for 0% -> 0%
where the time goes in v1:
time: 425 us; the launch traced here: 419 us
  waiting for transfers between devices  323 us (76%)
  matrix products  33.4 us (8%)
  between operations  20.7 us (5%)
  starting transfers between devices  14.6 us (3%)
  local copies, waits for them, and re-layouts  13.7 us (3%)
  other arithmetic  13.2 us (3%)
    psum x1, waiting for transfers between devices, per_device(): summed = lax.psum(stacked, 'wide')  266 us
    ppermute x10, waiting for transfers between devices, moved(): return lax.ppermute(value, axis, [(i, target(i)) for i in range(devices)])  57.7 us
    dot_general x5, matrix products, product(): return jnp.einsum('rtxy,tcyz->rcxz', lhs, rhs, precision=highest)  33.4 us
    ppermute x10, starting transfers between devices, moved(): return lax.ppermute(value, axis, [(i, target(i)) for i in range(devices)])  14.6 us
  transfers between devices with their start and end apart: 11, of which 5 were waited for; matrix products, arithmetic and copies ran while one was open for 9% of the time, Pallas kernels for 0%

profile of v1, /device:TPU:32, one launch (start us, length us, event | category | flops | bytes accessed | tf_op | source)
XLA Modules:
  0.0 418.8 jit_solution(2741778323685520183)
XLA Ops:
  6.5 1.9 copy.12
  8.5 0.1 copy.13
  8.6 1.6 bitcast_multiply_fusion.1
  10.1 1.5 collective-permute-start.3
  11.6 1.7 collective-permute-start.1
  13.4 0.1 copy.14
  13.5 4.0 bitcast_multiply_fusion
  17.5 1.1 dynamic-slice_bitcast_fusion.3
  18.6 1.7 collective-permute-start
  20.3 0.4 collective-permute-start.2
  20.7 1.6 collective-permute-start.6
  22.3 36.6 %collective-permute-done.3 = f32[4,8,128,128]{2,3,0,1:T(8,128)S(1)} collective-permute-done((f32[4,8,128,128]{2,3,0,1:T(8,128)}, f32[4,8,128,128]{2,3,0,1:T(8,128)S(1)}, u32[]{:S(2)}, u32[]{:S(2)}) %collective-permute-start.3) | collective-permute-done | bytes 2097184 | tf_op jit(solution)/shard_map/ppermute | solution.py:9
  58.9 0.1 slice.16
  59.0 0.4 collective-permute-start.5
  59.4 1.3 slice.17
  60.7 3.0 collective-permute-start.7
  63.7 1.6 collective-permute-start.4
  65.3 8.5 %fusion = f32[8,128,8,128,1]{3,1,4,2,0:T(8,128)S(1)} fusion(f32[4,4,128,128]{3,2,1,0:T(8,128)S(1)} %collective-permute-done, f32[4,4,128,128]{3,2,1,0:T(8,128)S(1)} %get-tuple-element.24, f32[4,8,128,128]{2,3,0,1:T(8,128)} %bitcast_multiply_fusion.1), kind=kOutput, calls=%fused_computation.5 | convolution fusion | flops 6442975232 | bytes 8388608 | tf_op jit(solution)/shard_map/rtxy,tcyz->rcxz/dot_general | solution.py:58
  73.8 8.7 %fusion.3 = f32[8,128,8,128,1]{3,1,4,2,0:T(8,128)S(1)} fusion(f32[4,4,128,128]{3,2,1,0:T(8,128)S(1)} %collective-permute-done.2, f32[4,4,128,128]{3,2,1,0:T(8,128)S(1)} %get-tuple-element.22, f32[4,8,128,128]{2,3,0,1:T(8,128)} %collective-permute-done.1), kind=kOutput, calls=%fused_computation.9 | convolution fusion | flops 6442975232 | bytes 8388608 | tf_op jit(solution)/shard_map/rtxy,tcyz->rcxz/dot_general | solution.py:58
  82.5 7.1 %collective-permute-done.6 = f32[4,4,128,128]{3,2,1,0:T(8,128)S(1)} collective-permute-done((f32[4,4,128,128]{3,2,1,0:T(8,128)S(1)}, f32[4,4,128,128]{3,2,1,0:T(8,128)S(1)}, u32[]{:S(2)}, u32[]{:S(2)}) %collective-permute-start.6) | collective-permute-done | bytes 1048608 | tf_op jit(solution)/shard_map/ppermute | solution.py:9
  89.7 3.6 fusion.13
  93.3 3.6 fusion.14
  96.9 13.6 %collective-permute-done.4 = f32[4,4,128,128]{3,2,1,0:T(8,128)S(1)} collective-permute-done((f32[4,4,128,128]{3,2,1,0:T(8,128)S(1)}, f32[4,4,128,128]{3,2,1,0:T(8,128)S(1)}, u32[]{:S(2)}, u32[]{:S(2)}) %collective-permute-start.4) | collective-permute-done | bytes 1048608 | tf_op jit(solution)/shard_map/ppermute | solution.py:9
  110.5 9.0 %maximum_add_fusion = f32[8,8,128,128]{2,3,0,1:T(8,128)} fusion(f32[8,4,128,128]{2,3,0,1:T(8,128)S(1)} %fusion.14, f32[8,4,128,128]{2,3,0,1:T(8,128)S(1)} %fusion.13, f32[8,128,8,128,1]{3,1,4,2,0:T(8,128)S(1)} %fusion.3, f32[8,128,8,128,1]{3,1,4,2,0:T(8,128)S(1)} %fusion, f32[4,4,128,128]{3,2,1,0:T(8,128)S(1)} %collective-permute-done.4, ...), kind=kOutput, calls=%fused_computation.1 | convolution fusion | flops 6447169536 | bytes 20971520 | tf_op jit(solution)/shard_map/rtxy,tcyz->rcxz/dot_general | solution.py:58
  119.5 5.4 %copy.15 = f32[8,8,128,128]{3,2,1,0:T(8,128)} copy(f32[8,8,128,128]{2,3,0,1:T(8,128)} %maximum_add_fusion) | data formatting | bytes 8388608 | tf_op jit(solution)/shard_map/add | solution.py:64
  124.9 0.7 copy-done.1
  125.5 1.6 collective-permute-start.8
  127.1 0.1 reshape.162
  127.2 0.1 reshape.145
  127.3 0.1 reduce.43
  127.5 0.7 and_reduce_fusion.6
  128.1 0.7 and_reduce_fusion.4
  128.8 0.1 reshape.139
  128.9 0.3 collective-permute-done.8
  129.1 0.1 reshape.163
  129.2 0.1 reshape.147
  129.3 0.1 reduce.57
  129.5 0.7 and_reduce_fusion.2
  131.3 0.7 and_reduce_fusion
  133.2 0.1 reshape.142
  134.5 0.6 and_reduce_fusion.3
  135.1 265.6 %all-reduce.2.cloned.1.call-done = f32[2,32,128,128]{3,2,1,0:T(8,128)} async-done(((f32[2,32,128,128]{3,2,1,0:T(8,128)}), f32[2,32,128,128]{3,2,1,0:T(8,128)}) %all-reduce.2.cloned.1.call-update) | async-done | bytes 4194320 | tf_op jit(solution)/shard_map/psum | solution.py:70
  400.7 2.6 fusion.23
  403.3 1.2 select_bitcast_fusion.1
  404.6 1.1 collective-permute-start.9
  405.6 0.7 and_reduce_fusion.7
  409.9 1.4 select_bitcast_fusion.3
  411.3 0.7 fusion.17
  (20 shorter events, 0.2 us)
Async XLA Ops:
  6.5 2.0 copy-start.2
  6.5 394.2 %all-reduce.2.cloned.1.call-start = ((), (), s32[]{:S(2)}) async-start(), calls=%async_computation | async-start | bytes 8388608 | tf_op jit(solution)/shard_map/psum | solution.py:70
  8.6 4.8 %copy-start = (s32[4,8,1,4]{1,3,2,0:T(4,128)S(1)}, s32[4,8,1,4]{1,3,2,0:T(4,128)}, u32[]{:S(2)}) copy-start(s32[4,8,1,4]{1,3,2,0:T(4,128)} %param.6) | copy-start | bytes 1540
  10.1 48.8 %collective-permute-start.3 = (f32[4,8,128,128]{2,3,0,1:T(8,128)}, f32[4,8,128,128]{2,3,0,1:T(8,128)S(1)}, u32[]{:S(2)}, u32[]{:S(2)}) collective-permute-start(f32[4,8,128,128]{2,3,0,1:T(8,128)} %bitcast_multiply_fusion.1), channel_id=1, source_target_pairs={{0,32},{32,64},{64,96},{96,0},{128,160},{160,192},{192,224},{224,1... | collective-permute-start | bytes 6291464 | tf_op jit(solution)/shard_map/ppermute | solution.py:9
  11.6 47.7 %collective-permute-start.1 = (f32[4,8,128,128]{2,3,0,1:T(8,128)}, f32[4,8,128,128]{2,3,0,1:T(8,128)}, u32[]{:S(2)}, u32[]{:S(2)}) collective-permute-start(f32[4,8,128,128]{2,3,0,1:T(8,128)} %bitcast_multiply_fusion.1), channel_id=1, source_target_pairs={{0,96},{32,0},{64,32},{96,64},{128,224},{160,128},{192,160},{224,1... | collective-permute-start | bytes 6291464 | tf_op jit(solution)/shard_map/ppermute | solution.py:9
  18.6 45.1 %collective-permute-start = (f32[4,4,128,128]{3,2,1,0:T(8,128)S(1)}, f32[4,4,128,128]{3,2,1,0:T(8,128)S(1)}, u32[]{:S(2)}, u32[]{:S(2)}) collective-permute-start(f32[4,4,128,128]{3,2,1,0:T(8,128)S(1)} %get-tuple-element.23), channel_id=1, source_target_pairs={{0,128},{32,160},{64,192},{96,224},{128,0},{160,32},{192,64},{224,... | collective-permute-start | bytes 3145736 | tf_op jit(solution)/shard_map/ppermute | solution.py:9
  20.3 53.5 %collective-permute-start.2 = (f32[4,4,128,128]{3,2,1,0:T(8,128)S(1)}, f32[4,4,128,128]{3,2,1,0:T(8,128)S(1)}, u32[]{:S(2)}, u32[]{:S(2)}) collective-permute-start(f32[4,4,128,128]{3,2,1,0:T(8,128)S(1)} %get-tuple-element.21), channel_id=1, source_target_pairs={{0,128},{32,160},{64,192},{96,224},{128,0},{160,32},{192,64},{224,... | collective-permute-start | bytes 3145736 | tf_op jit(solution)/shard_map/ppermute | solution.py:9
  20.7 68.9 %collective-permute-start.6 = (f32[4,4,128,128]{3,2,1,0:T(8,128)S(1)}, f32[4,4,128,128]{3,2,1,0:T(8,128)S(1)}, u32[]{:S(2)}, u32[]{:S(2)}) collective-permute-start(f32[4,4,128,128]{3,2,1,0:T(8,128)S(1)} %get-tuple-element.18), channel_id=1, source_target_pairs={{0,128},{32,160},{64,192},{96,224},{128,0},{160,32},{192,64},{224,... | collective-permute-start | bytes 3145736 | tf_op jit(solution)/shard_map/ppermute | solution.py:9
  59.0 30.7 %collective-permute-start.5 = (f32[4,4,128,128]{2,3,0,1:T(8,128)S(1)}, f32[4,4,128,128]{2,3,0,1:T(8,128)S(1)}, u32[]{:S(2)}, u32[]{:S(2)}) collective-permute-start(f32[4,4,128,128]{2,3,0,1:T(8,128)S(1)} %slice.16), channel_id=1, source_target_pairs={{0,32},{32,64},{64,96},{96,0},{128,160},{160,192},{192,224},{224,1... | collective-permute-start | bytes 3145736 | tf_op jit(solution)/shard_map/ppermute | solution.py:9
  60.7 32.6 %collective-permute-start.7 = (f32[4,4,128,128]{2,3,0,1:T(8,128)S(1)}, f32[4,4,128,128]{2,3,0,1:T(8,128)S(1)}, u32[]{:S(2)}, u32[]{:S(2)}) collective-permute-start(f32[4,4,128,128]{2,3,0,1:T(8,128)S(1)} %slice.17), channel_id=1, source_target_pairs={{0,96},{32,0},{64,32},{96,64},{128,224},{160,128},{192,160},{224,1... | collective-permute-start | bytes 3145736 | tf_op jit(solution)/shard_map/ppermute | solution.py:9
  63.7 46.7 %collective-permute-start.4 = (f32[4,4,128,128]{3,2,1,0:T(8,128)S(1)}, f32[4,4,128,128]{3,2,1,0:T(8,128)S(1)}, u32[]{:S(2)}, u32[]{:S(2)}) collective-permute-start(f32[4,4,128,128]{3,2,1,0:T(8,128)S(1)} %get-tuple-element.20), channel_id=1, source_target_pairs={{0,128},{32,160},{64,192},{96,224},{128,0},{160,32},{192,64},{224,... | collective-permute-start | bytes 3145736 | tf_op jit(solution)/shard_map/ppermute | solution.py:9
  124.9 0.7 copy-start.1
  125.5 3.6 collective-permute-start.8
  404.6 6.8 %collective-permute-start.9 = (f32[2,128,128]{2,1,0:T(8,128)S(1)}, f32[2,128,128]{2,1,0:T(8,128)S(1)}, u32[]{:S(2)}, u32[]{:S(2)}) collective-permute-start(f32[2,128,128]{2,1,0:T(8,128)S(1)} %pad_maximum_fusion), channel_id=1, source_target_pairs={{0,128},{32,160},{64,192},{96,224},{128,0},{160,32},{192,64},{224,... | collective-permute-start | bytes 393224 | tf_op jit(solution)/shard_map/ppermute | solution.py:9
Sparse Core Ops, SparseCore 0:
  125.0 275.6 all-reduce.1
